TPU v7x, 512 devices: a whole 4x4x16 slice. The times are simulated.
512 devices in a mesh: col: 4 (over x_lo, core), gx: 16 (over z), gy: 8 (over x_hi, y).
Axes of the slice: x: 4 (x_hi: 2, x_lo: 2; x = x_hi * 2 + x_lo), y: 4, z: 16, core: 2. Of those that a mesh axis runs over, the one named last changes fastest.
Arguments:
- volume: float32 [32, 8, 64, 1024], P('col', None, 'gx', 'gy'), may hold values from -6 to 6
- filters: float32 [32, 32, 3, 3, 3], P('col'), may hold values from -0.21875 to 0.21875
- upstream: float32 [32, 8, 64, 1024], P('col', None, 'gx', 'gy'), may hold values from -6 to 6
Outputs:
- response: float32 [32, 8, 64, 1024], P('col', None, 'gx', 'gy')
- input_grad: float32 [32, 8, 64, 1024], P('col', None, 'gx', 'gy')
- filter_grad: float32 [32, 32, 3, 3, 3], P('col')
All inputs are finite; a program needn't handle non-finite values.
Results may differ from a plain program's by a relative error of at most 0.0003.
Values sent between devices are 32-bit elements; how exact they have to be, the bound alone decides.
No kernel may reach another device: no remote copies, remote signals or barrier semaphores. Data moves between devices by JAX's collectives and lax.ppermute only.
A program may use at most 64 MiB of HBM per device.

v0:
```python
import jax
import jax.numpy as jnp
from jax import lax
from jax.sharding import PartitionSpec as P


def with_halo(block, sides, width):
    for axis, dim in sides:
        count = lax.axis_size(axis)
        forward = [(i, i + 1) for i in range(count - 1)]
        backward = [(target, source) for source, target in forward]
        low = lax.ppermute(
            lax.slice_in_dim(block, block.shape[dim] - width, None, axis=dim), axis, forward
        )
        high = lax.ppermute(lax.slice_in_dim(block, 0, width, axis=dim), axis, backward)
        block = jnp.concatenate([low, block, high], axis=dim)
    return block


def pad_depth(field):
    return jnp.pad(field, ((0, 0), (1, 1), (0, 0), (0, 0)))


def forward_conv(padded, weights, planes, rows_x, rows_y):
    output = jnp.zeros((weights.shape[0], planes, rows_x, rows_y), jnp.float32)
    for depth in range(3):
        for across in range(3):
            for along in range(3):
                window = padded[
                    :, depth : depth + planes, across : across + rows_x, along : along + rows_y
                ]
                output = output + jnp.einsum(
                    "oc,czxy->ozxy",
                    weights[:, :, depth, across, along],
                    window,
                    precision=lax.Precision.HIGHEST,
                )
    return output


def backward_conv(padded_up, weights, planes, rows_x, rows_y):
    output = jnp.zeros((weights.shape[1], planes, rows_x, rows_y), jnp.float32)
    for depth in range(3):
        for across in range(3):
            for along in range(3):
                window = padded_up[
                    :,
                    2 - depth : 2 - depth + planes,
                    2 - across : 2 - across + rows_x,
                    2 - along : 2 - along + rows_y,
                ]
                output = output + jnp.einsum(
                    "oc,ozxy->czxy",
                    weights[:, :, depth, across, along],
                    window,
                    precision=lax.Precision.HIGHEST,
                )
    return output


def weight_terms(cotangent, padded, planes, rows_x, rows_y):
    pieces = []
    for depth in range(3):
        for across in range(3):
            for along in range(3):
                window = padded[
                    :, depth : depth + planes, across : across + rows_x, along : along + rows_y
                ]
                pieces.append(
                    jnp.einsum("ozxy,czxy->oc", cotangent, window, precision=lax.Precision.HIGHEST)
                )
    stacked = jnp.stack(pieces, axis=-1)
    return stacked.reshape(stacked.shape[0], stacked.shape[1], 3, 3, 3)


def shards(volume, filters, upstream):
    planes, rows_x, rows_y = (volume.shape[1], volume.shape[2], volume.shape[3])
    own_inputs = volume.shape[0]
    scale = (planes * rows_x * lax.axis_size("gx") * rows_y * lax.axis_size("gy")) ** (-0.5)
    gathered = lax.all_gather(volume, "col", axis=0, tiled=True)
    padded = pad_depth(with_halo(gathered, (("gx", 2), ("gy", 3)), 1))
    response = forward_conv(padded, filters, planes, rows_x, rows_y)
    all_rows = lax.all_gather(filters, "col", axis=0, tiled=True)
    all_upstream = lax.all_gather(upstream, "col", axis=0, tiled=True)
    padded_up = pad_depth(with_halo(all_upstream, (("gx", 2), ("gy", 3)), 1))
    first = lax.axis_index("col") * own_inputs
    own_filters = lax.dynamic_slice_in_dim(all_rows, first, own_inputs, 1)
    input_grad = backward_conv(padded_up, own_filters, planes, rows_x, rows_y)
    local_grad = weight_terms(upstream, padded, planes, rows_x, rows_y)
    ncol = lax.axis_size("col")
    flat = local_grad.reshape(-1, 128)
    slots = jnp.zeros((ncol,) + flat.shape, jnp.float32)
    slots = lax.dynamic_update_index_in_dim(slots, flat, lax.axis_index("col"), 0)
    summed = lax.psum(slots, ("col", "gx", "gy"))
    total_grad = summed[lax.axis_index("col")].reshape(local_grad.shape)
    return (response, input_grad, total_grad * scale)


def solution(mesh):
    placed = (
        P("col", None, "gx", "gy"),
        P("col", None, None, None, None),
        P("col", None, "gx", "gy"),
    )
    return jax.shard_map(
        shards,
        mesh=mesh,
        in_specs=placed,
        out_specs=(
            P("col", None, "gx", "gy"),
            P("col", None, "gx", "gy"),
            P("col", None, None, None, None),
        ),
        check_vma=False,
    )
```

profile of v0, /device:TPU:1, one launch (start us, length us, event | category | flops | bytes accessed | tf_op | source)
XLA Modules:
  0.0 655.5 jit_solution(1451040845485001192)
XLA Ops:
  8.2 13.2 %all_gather.9 = f32[32,8,4,128]{3,0,2,1:T(8,128)S(1)} all-gather(f32[8,8,4,128]{3,0,2,1:T(8,128)S(1)} %copy.126), channel_id=1, replica_groups=mesh['col'=4,'gx'=16,'gy'=8] {'col'}, dimensions={0}, use_global_device_ids=true | all-gather | bytes 655360 | tf_op jit(solution)/shard_map/all_gather | solution.py:80
  22.1 1.3 collective-permute-start
  23.4 1.3 collective-permute-start.1
  25.7 7.3 %all_gather.11 = f32[32,8,4,128]{3,0,2,1:T(8,128)S(1)} all-gather(f32[8,8,4,128]{3,0,2,1:T(8,128)S(1)} %copy.134), channel_id=1, replica_groups=mesh['col'=4,'gx'=16,'gy'=8] {'col'}, dimensions={0}, use_global_device_ids=true | all-gather | bytes 655360 | tf_op jit(solution)/shard_map/all_gather | solution.py:84
  33.7 4.6 collective-permute-start.4
  38.3 1.3 collective-permute-start.5
  39.6 6.8 %all_gather.10 = f32[32,32,3,3,3]{1,0,4,3,2:T(8,128)S(1)} all-gather(f32[8,32,3,3,3]{1,0,4,3,2:T(8,128)S(1)} %copy-done.66), channel_id=1, replica_groups=mesh['col'=4,'gx'=16,'gy'=8] {'col'}, dimensions={0}, use_global_device_ids=true | all-gather | bytes 138240 | tf_op jit(solution)/shard_map/all_gather | solution.py:83
  49.9 1.9 collective-permute-start.2
  52.8 1.3 collective-permute-start.3
  56.0 1.2 fusion.310
  57.2 2.1 copy.135
  59.2 4.6 collective-permute-start.6
  64.8 1.8 collective-permute-start.7
  66.6 1.7 fusion.208
  68.3 2.0 fusion.116
  70.4 2.0 fusion.112
  75.6 2.9 pad_maximum_fusion.9
  78.5 2.1 select_maximum_fusion.2
  81.7 2.0 copy.138
  83.7 1.9 select_maximum_fusion
  85.6 1.3 fusion.120
  89.1 1.2 fusion.122
  90.3 1.2 fusion.126
  94.9 1.2 fusion.80
  96.1 1.3 fusion.83
  97.4 1.3 fusion.86
  98.7 1.2 fusion.100
  99.9 1.2 fusion.102
  101.1 1.2 fusion.106
  102.3 1.2 fusion.94
  105.8 1.2 fusion.108
  108.1 1.4 fusion.96
  109.4 1.2 fusion.110
  110.6 1.3 fusion.114
  111.9 4.3 fusion.309
  116.2 1.8 fusion.212
  118.0 1.8 fusion.214
  119.9 1.7 fusion.216
  121.6 1.8 fusion.218
  123.4 1.8 fusion.220
  125.2 1.7 fusion.222
  127.0 1.9 fusion.224
  128.9 1.9 fusion.226
  130.8 1.8 convolution_bitcast_fusion.6
  132.6 1.9 convolution_bitcast_fusion.7
  134.5 1.9 convolution_bitcast_fusion.8
  136.4 1.8 convolution_bitcast_fusion.9
  139.3 1.8 fusion.210
  152.7 1.8 fusion.206
  155.7 1.8 fusion.204
  159.8 1.8 convolution_bitcast_fusion.10
  176.5 1.7 copy.195
  178.1 1.7 broadcast_in_dim.8
  180.5 1.4 constant_dynamic-update-slice_fusion.10
  182.0 2.0 fusion.47
  188.6 1.3 fusion.14
  189.9 1.2 fusion.13
  191.2 1.2 fusion.12
  192.5 1.2 fusion.11
  193.8 2.1 fusion.48
  196.0 1.3 fusion.49
  197.3 1.2 fusion.10
  199.9 445.2 %all-reduce.4.cloned.1.call-done = f32[4,54,128]{2,1,0:T(8,128)} async-done(((f32[4,54,128]{2,1,0:T(8,128)}), f32[4,54,128]{2,1,0:T(8,128)}) %all-reduce.4.cloned.1.call-update) | async-done | bytes 110608 | tf_op jit(solution)/shard_map/psum | solution.py:94
  646.7 1.6 copy.198
  (206 shorter events, 62.9 us)
Async XLA Ops:
  7.2 32.4 %copy-start.66 = (f32[8,32,3,3,3]{1,0,4,3,2:T(8,128)S(1)}, f32[8,32,3,3,3]{1,0,4,3,2:T(8,128)}, u32[]{:S(2)}) copy-start(f32[8,32,3,3,3]{1,0,4,3,2:T(8,128)} %param.4) | copy-start | bytes 82948
  7.2 637.9 %all-reduce.4.cloned.1.call-start = ((), (), s32[]{:S(2)}) async-start(), calls=%async_computation | async-start | bytes 229376 | tf_op jit(solution)/shard_map/psum | solution.py:94
  21.4 26.4 %copy-start.3 = (f32[32,8,4,128]{3,0,2,1:T(8,128)}, f32[32,8,4,128]{3,0,2,1:T(8,128)S(1)}, u32[]{:S(2)}) copy-start(f32[32,8,4,128]{3,0,2,1:T(8,128)S(1)} %all_gather.9) | copy-start | bytes 1572868
  22.1 25.5 %collective-permute-start = (f32[32,8,1,128]{3,0,2,1:T(8,128)S(1)}, f32[32,8,1,128]{3,0,2,1:T(8,128)S(1)}, u32[]{:S(2)}, u32[]{:S(2)}) collective-permute-start(f32[32,8,1,128]{3,0,2,1:T(8,128)S(1)} %get-tuple-element.49), channel_id=1, source_target_pairs={{0,8},{8,16},{16,24},{24,32},{32,40},{40,48},{48,56},{56,64},{64,7... | collective-permute-start | bytes 393224 | tf_op jit(solution)/shard_map/ppermute | solution.py:12
  23.4 24.4 %collective-permute-start.1 = (f32[32,8,1,128]{3,0,2,1:T(8,128)}, f32[32,8,1,128]{3,0,2,1:T(8,128)S(1)}, u32[]{:S(2)}, u32[]{:S(2)}) collective-permute-start(f32[32,8,1,128]{3,0,2,1:T(8,128)} %get-tuple-element.48), channel_id=1, source_target_pairs={{8,0},{16,8},{24,16},{32,24},{40,32},{48,40},{56,48},{64,56},{72,6... | collective-permute-start | bytes 393224 | tf_op jit(solution)/shard_map/ppermute | solution.py:15
  33.7 20.4 %collective-permute-start.4 = (f32[32,8,1,128]{3,0,2,1:T(8,128)}, f32[32,8,1,128]{3,0,2,1:T(8,128)}, u32[]{:S(2)}, u32[]{:S(2)}) collective-permute-start(f32[32,8,1,128]{3,0,2,1:T(8,128)} %get-tuple-element.44), channel_id=1, source_target_pairs={{0,8},{8,16},{16,24},{24,32},{32,40},{40,48},{48,56},{56,64},{64,7... | collective-permute-start | bytes 393224 | tf_op jit(solution)/shard_map/ppermute | solution.py:12
  38.3 16.7 %collective-permute-start.5 = (f32[32,8,1,128]{3,0,2,1:T(8,128)}, f32[32,8,1,128]{3,0,2,1:T(8,128)}, u32[]{:S(2)}, u32[]{:S(2)}) collective-permute-start(f32[32,8,1,128]{3,0,2,1:T(8,128)} %get-tuple-element.43), channel_id=1, source_target_pairs={{8,0},{16,8},{24,16},{32,24},{40,32},{48,40},{56,48},{64,56},{72,6... | collective-permute-start | bytes 393224 | tf_op jit(solution)/shard_map/ppermute | solution.py:15
  49.9 22.5 %collective-permute-start.2 = (f32[32,8,6,1]{0,1,3,2:T(8,128)}, f32[32,8,6,1]{0,1,3,2:T(8,128)}, u32[]{:S(2)}, u32[]{:S(2)}) collective-permute-start(f32[32,8,6,1]{0,1,3,2:T(8,128)} %copy.127), channel_id=1, source_target_pairs={{0,1},{1,2},{2,3},{3,4},{4,5},{5,6},{6,7},{8,9},{9,10},{10,11},{11... | collective-permute-start | bytes 18440 | tf_op jit(solution)/shard_map/ppermute | solution.py:12
  52.8 20.7 %collective-permute-start.3 = (f32[32,8,6,1]{0,1,3,2:T(8,128)}, f32[32,8,6,1]{0,1,3,2:T(8,128)}, u32[]{:S(2)}, u32[]{:S(2)}) collective-permute-start(f32[32,8,6,1]{0,1,3,2:T(8,128)} %copy.128), channel_id=1, source_target_pairs={{1,0},{2,1},{3,2},{4,3},{5,4},{6,5},{7,6},{9,8},{10,9},{11,10},{12... | collective-permute-start | bytes 18440 | tf_op jit(solution)/shard_map/ppermute | solution.py:15
  56.0 10.6 %copy-start.20 = (f32[32,8,5,128]{3,0,2,1:T(8,128)S(1)}, f32[32,8,5,128]{3,0,2,1:T(8,128)}, u32[]{:S(2)}) copy-start(f32[32,8,5,128]{3,0,2,1:T(8,128)} %copy-done.19) | copy-start | bytes 1966084
  59.2 21.3 %collective-permute-start.6 = (f32[32,8,6,1]{0,1,3,2:T(8,128)}, f32[32,8,6,1]{0,1,3,2:T(8,128)}, u32[]{:S(2)}, u32[]{:S(2)}) collective-permute-start(f32[32,8,6,1]{0,1,3,2:T(8,128)} %copy.135), channel_id=1, source_target_pairs={{0,1},{1,2},{2,3},{3,4},{4,5},{5,6},{6,7},{8,9},{9,10},{10,11},{11... | collective-permute-start | bytes 18440 | tf_op jit(solution)/shard_map/ppermute | solution.py:12
  64.8 16.9 %collective-permute-start.7 = (f32[32,8,6,1]{0,1,3,2:T(8,128)}, f32[32,8,6,1]{0,1,3,2:T(8,128)}, u32[]{:S(2)}, u32[]{:S(2)}) collective-permute-start(f32[32,8,6,1]{0,1,3,2:T(8,128)} %copy.136), channel_id=1, source_target_pairs={{1,0},{2,1},{3,2},{4,3},{5,4},{6,5},{7,6},{9,8},{10,9},{11,10},{12... | collective-permute-start | bytes 18440 | tf_op jit(solution)/shard_map/ppermute | solution.py:15
  85.5 22.5 %copy-start.1 = (f32[32,10,6,130]{3,0,2,1:T(8,128)}, f32[32,10,6,130]{3,0,2,1:T(8,128)S(1)}, u32[]{:S(2)}) copy-start(f32[32,10,6,130]{3,0,2,1:T(8,128)S(1)} %select_maximum_fusion) | copy-start | bytes 2995204
  127.0 11.2 %copy-start = (f32[8,8,4,128]{3,2,1,0:T(4,128)S(1)}, f32[8,8,4,128]{3,2,1,0:T(4,128)}, u32[]{:S(2)}) copy-start(f32[8,8,4,128]{3,2,1,0:T(4,128)} %param.5) | copy-start | bytes 393220
  127.0 11.2 %copy-start.33 = (f32[32,8,4,128]{3,0,2,1:T(8,128)S(1)}, f32[32,8,4,128]{3,0,2,1:T(8,128)}, u32[]{:S(2)}) copy-start(f32[32,8,4,128]{3,0,2,1:T(8,128)} %get-tuple-element.29) | copy-start | bytes 1572868
  128.9 10.4 %copy-start.13 = (f32[32,8,4,128]{3,0,2,1:T(8,128)S(1)}, f32[32,8,4,128]{3,0,2,1:T(8,128)}, u32[]{:S(2)}) copy-start(f32[32,8,4,128]{3,0,2,1:T(8,128)} %get-tuple-element.31) | copy-start | bytes 1572868
  130.8 10.3 %copy-start.32 = (f32[32,8,4,128]{3,0,2,1:T(8,128)S(1)}, f32[32,8,4,128]{3,0,2,1:T(8,128)}, u32[]{:S(2)}) copy-start(f32[32,8,4,128]{3,0,2,1:T(8,128)} %get-tuple-element.28) | copy-start | bytes 1572868
  132.6 9.7 %copy-start.31 = (f32[32,8,4,128]{3,0,2,1:T(8,128)S(1)}, f32[32,8,4,128]{3,0,2,1:T(8,128)}, u32[]{:S(2)}) copy-start(f32[32,8,4,128]{3,0,2,1:T(8,128)} %get-tuple-element.27) | copy-start | bytes 1572868
  134.5 8.9 %copy-start.30 = (f32[32,8,4,128]{3,0,2,1:T(8,128)S(1)}, f32[32,8,4,128]{3,0,2,1:T(8,128)}, u32[]{:S(2)}) copy-start(f32[32,8,4,128]{3,0,2,1:T(8,128)} %get-tuple-element.26) | copy-start | bytes 1572868
  136.3 8.2 %copy-start.29 = (f32[32,8,4,128]{3,0,2,1:T(8,128)S(1)}, f32[32,8,4,128]{3,0,2,1:T(8,128)}, u32[]{:S(2)}) copy-start(f32[32,8,4,128]{3,0,2,1:T(8,128)} %get-tuple-element.25) | copy-start | bytes 1572868
  138.1 7.5 %copy-start.28 = (f32[32,8,4,128]{3,0,2,1:T(8,128)S(1)}, f32[32,8,4,128]{3,0,2,1:T(8,128)}, u32[]{:S(2)}) copy-start(f32[32,8,4,128]{3,0,2,1:T(8,128)} %get-tuple-element.24) | copy-start | bytes 1572868
  139.3 7.5 %copy-start.27 = (f32[32,8,4,128]{3,0,2,1:T(8,128)S(1)}, f32[32,8,4,128]{3,0,2,1:T(8,128)}, u32[]{:S(2)}) copy-start(f32[32,8,4,128]{3,0,2,1:T(8,128)} %get-tuple-element.23) | copy-start | bytes 1572868
  141.1 6.9 %copy-start.26 = (f32[32,8,4,128]{3,0,2,1:T(8,128)S(1)}, f32[32,8,4,128]{3,0,2,1:T(8,128)}, u32[]{:S(2)}) copy-start(f32[32,8,4,128]{3,0,2,1:T(8,128)} %get-tuple-element.22) | copy-start | bytes 1572868
  142.2 6.9 %copy-start.25 = (f32[32,8,4,128]{3,0,2,1:T(8,128)S(1)}, f32[32,8,4,128]{3,0,2,1:T(8,128)}, u32[]{:S(2)}) copy-start(f32[32,8,4,128]{3,0,2,1:T(8,128)} %get-tuple-element.21) | copy-start | bytes 1572868
  144.5 7.0 %copy-start.21 = (f32[32,8,5,128]{3,0,2,1:T(8,128)S(1)}, f32[32,8,5,128]{3,0,2,1:T(8,128)}, u32[]{:S(2)}) copy-start(f32[32,8,5,128]{3,0,2,1:T(8,128)} %copy-done.19) | copy-start | bytes 1966084
  145.7 7.1 %copy-start.12 = (f32[32,8,4,128]{3,0,2,1:T(8,128)S(1)}, f32[32,8,4,128]{3,0,2,1:T(8,128)}, u32[]{:S(2)}) copy-start(f32[32,8,4,128]{3,0,2,1:T(8,128)} %get-tuple-element.39) | copy-start | bytes 1572868
  147.9 7.7 %copy-start.11 = (f32[32,8,4,128]{3,0,2,1:T(8,128)S(1)}, f32[32,8,4,128]{3,0,2,1:T(8,128)}, u32[]{:S(2)}) copy-start(f32[32,8,4,128]{3,0,2,1:T(8,128)} %get-tuple-element.32) | copy-start | bytes 1572868
  150.2 8.4 %copy-start.4 = (f32[32,8,4,128]{3,0,2,1:T(8,128)S(1)}, f32[32,8,4,128]{3,0,2,1:T(8,128)}, u32[]{:S(2)}) copy-start(f32[32,8,4,128]{3,0,2,1:T(8,128)} %copy-done.3) | copy-start | bytes 1572868
  151.6 8.2 %copy-start.10 = (f32[32,8,4,128]{3,0,2,1:T(8,128)S(1)}, f32[32,8,4,128]{3,0,2,1:T(8,128)}, u32[]{:S(2)}) copy-start(f32[32,8,4,128]{3,0,2,1:T(8,128)} %get-tuple-element.38) | copy-start | bytes 1572868
  152.7 8.8 %copy-start.14 = (f32[32,8,4,128]{3,0,2,1:T(8,128)S(1)}, f32[32,8,4,128]{3,0,2,1:T(8,128)}, u32[]{:S(2)}) copy-start(f32[32,8,4,128]{3,0,2,1:T(8,128)} %get-tuple-element.40) | copy-start | bytes 1572868
  154.5 8.2 %copy-start.8 = (f32[32,8,4,128]{3,0,2,1:T(8,128)S(1)}, f32[32,8,4,128]{3,0,2,1:T(8,128)}, u32[]{:S(2)}) copy-start(f32[32,8,4,128]{3,0,2,1:T(8,128)} %get-tuple-element.30) | copy-start | bytes 1572868
  155.7 8.2 %copy-start.17 = (f32[32,8,5,128]{3,0,2,1:T(8,128)S(1)}, f32[32,8,5,128]{3,0,2,1:T(8,128)}, u32[]{:S(2)}) copy-start(f32[32,8,5,128]{3,0,2,1:T(8,128)} %copy-done.16) | copy-start | bytes 1966084
  158.6 7.5 %copy-start.24 = (f32[32,8,4,128]{3,0,2,1:T(8,128)S(1)}, f32[32,8,4,128]{3,0,2,1:T(8,128)}, u32[]{:S(2)}) copy-start(f32[32,8,4,128]{3,0,2,1:T(8,128)} %get-tuple-element.20) | copy-start | bytes 1572868
  159.8 7.5 %copy-start.23 = (f32[32,8,4,128]{3,0,2,1:T(8,128)S(1)}, f32[32,8,4,128]{3,0,2,1:T(8,128)}, u32[]{:S(2)}) copy-start(f32[32,8,4,128]{3,0,2,1:T(8,128)} %get-tuple-element.19) | copy-start | bytes 1572868
  161.6 6.9 %copy-start.22 = (f32[32,8,4,128]{3,0,2,1:T(8,128)S(1)}, f32[32,8,4,128]{3,0,2,1:T(8,128)}, u32[]{:S(2)}) copy-start(f32[32,8,4,128]{3,0,2,1:T(8,128)} %get-tuple-element.18) | copy-start | bytes 1572868
  181.9 5.4 copy-start.18
  181.9 5.4 copy-start.36
  181.9 5.4 copy-start.37
  181.9 5.4 copy-start.38
  182.0 5.4 copy-start.39
  182.0 5.4 copy-start.40
  188.4 5.2 copy-start.41
  188.4 5.2 copy-start.42
  188.5 5.2 copy-start.43
  188.5 5.2 copy-start.44
  188.5 5.2 copy-start.55
  188.5 5.2 copy-start.56
  188.5 5.2 copy-start.57
  188.5 5.2 copy-start.58
  188.5 5.2 copy-start.59
  188.5 5.2 copy-start.60
  188.5 5.2 copy-start.61
  188.5 5.2 copy-start.62
  188.6 5.2 copy-start.65
  191.1 4.8 copy-start.45
  191.1 4.8 copy-start.46
  191.1 4.8 copy-start.47
  191.1 4.8 copy-start.48
  191.1 4.8 copy-start.49
  191.1 4.8 copy-start.50
  191.2 4.8 copy-start.51
  191.2 4.8 copy-start.52
  191.2 4.8 copy-start.53
  191.2 4.8 copy-start.54
  (12 other events, 31.0 us)
Sparse Core Ops, SparseCore 0:
  182.0 463.0 all-reduce.3
where the time goes:
time: 660 us; the launch traced here: 655 us
  waiting for transfers between devices  445 us (67%)
  matrix products  109 us (17%)
  local copies, waits for them, and re-layouts  32.7 us (5%)
  blocking collectives  27.3 us (4%)
  starting transfers between devices  18.1 us (3%)
  between operations  15.4 us (2%)
  other arithmetic  7.59 us (1%)
    psum x1, waiting for transfers between devices, shards(): summed = lax.psum(slots, ('col', 'gx', 'gy'))  445 us
    dot_general x27, matrix products, forward_conv(): jnp.einsum('oc,czxy->ozxy', weights[:, :, depth, across, along], window,...  43.3 us
    dot_general x27, matrix products, backward_conv(): jnp.einsum('oc,ozxy->czxy', weights[:, :, depth, across, along], window,...  35 us
    dot_general x27, matrix products, weight_terms(): jnp.einsum('ozxy,czxy->oc', cotangent, window, precision=lax.Precision.HI...  30.8 us
  transfers between devices with their start and end apart: 9, of which 1 were waited for; matrix products, arithmetic and copies ran while one was open for 7% of the time, Pallas kernels for 0%

commit v1 on v0

--- a/solution.py
+++ b/solution.py
@@ -2,6 +2,13 @@
 import jax.numpy as jnp
 from jax import lax
 from jax.sharding import PartitionSpec as P
+
+
+def swapped_in(x, axis, dim):
+    size = lax.axis_size(axis)
+    blocks = jnp.stack([x for _ in range(size)])
+    blocks = lax.all_to_all(blocks, axis, split_axis=0, concat_axis=0)
+    return jnp.concatenate(blocks, axis=dim)
 
 
 def with_halo(block, sides, width):
@@ -77,7 +84,7 @@
     planes, rows_x, rows_y = (volume.shape[1], volume.shape[2], volume.shape[3])
     own_inputs = volume.shape[0]
     scale = (planes * rows_x * lax.axis_size("gx") * rows_y * lax.axis_size("gy")) ** (-0.5)
-    gathered = lax.all_gather(volume, "col", axis=0, tiled=True)
+    gathered = swapped_in(volume, "col", 0)
     padded = pad_depth(with_halo(gathered, (("gx", 2), ("gy", 3)), 1))
     response = forward_conv(padded, filters, planes, rows_x, rows_y)
     all_rows = lax.all_gather(filters, "col", axis=0, tiled=True)

time: 660 us -> 637 us (0.965)
  matrix products: 109 us -> 82.1 us
  waiting for transfers between devices: 445 us -> 461 us
  starting transfers between devices: 18.1 us -> 27.2 us
  local copies, waits for them, and re-layouts: 32.7 us -> 23.9 us
  blocking collectives: 27.3 us -> 19.1 us
    dot_general x27, matrix products: 35 us -> 16.8 us  [backward_conv(): jnp.einsum('oc,ozxy->czxy', weights[:, :, depth, across, along], window,...]
    all_gather x1 -> x0, blocking collectives: 13.2 us -> none  [shards(): gathered = lax.all_gather(volume, 'col', axis=0, tiled=True)]
    psum x1, waiting for transfers between devices: 445 us -> 458 us  [shards(): summed = lax.psum(slots, ('col', 'gx', 'gy'))]
    all_to_all x0 -> x1, starting transfers between devices: none -> 10.3 us  [swapped_in(): blocks = lax.all_to_all(blocks, axis, split_axis=0, concat_axis=0)]
    dot_general x27, matrix products: 43.3 us -> 34.2 us  [forward_conv(): jnp.einsum('oc,czxy->ozxy', weights[:, :, depth, across, along], window,...]
  transfers between devices with their start and end apart: 9 -> 10, of which waited for: 1 -> 2; matrix products, arithmetic and copies ran while one was open for 7% -> 5% of each run, Pallas kernels for 0% -> 0%
where the time goes in v1:
time: 637 us; the launch traced here: 634 us
  waiting for transfers between devices  461 us (72%)
  matrix products  82.1 us (13%)
  starting transfers between devices  27.2 us (4%)
  local copies, waits for them, and re-layouts  23.9 us (4%)
  blocking collectives  19.1 us (3%)
  between operations  15.1 us (2%)
    psum x1, waiting for transfers between devices, shards(): summed = lax.psum(slots, ('col', 'gx', 'gy'))  458 us
    dot_general x27, matrix products, forward_conv(): jnp.einsum('oc,czxy->ozxy', weights[:, :, depth, across, along], window,...  34.2 us
    dot_general x27, matrix products, weight_terms(): jnp.einsum('ozxy,czxy->oc', cotangent, window, precision=lax.Precision.HI...  31.1 us
    dot_general x27, matrix products, backward_conv(): jnp.einsum('oc,ozxy->czxy', weights[:, :, depth, across, along], window,...  16.8 us
  transfers between devices with their start and end apart: 10, of which 2 were waited for; matrix products, arithmetic and copies ran while one was open for 5% of the time, Pallas kernels for 0%

profile of v1, /device:TPU:1, one launch (start us, length us, event | category | flops | bytes accessed | tf_op | source)
XLA Modules:
  0.0 633.7 jit_solution(12122410551650406626)
XLA Ops:
  9.1 10.3 %all-to-all-start = ((f32[4,8,8,4,128]{4,1,3,2,0:T(8,128)}), f32[4,8,8,4,128]{4,1,3,2,0:T(8,128)S(1)}, u32[]{:S(2)}, u32[]{:S(2)}) async-start(f32[4,8,8,4,128]{4,1,3,2,0:T(8,128)} %stack.91), calls=%async_computation | async-start | bytes 1048576 | tf_op jit(solution)/shard_map/all_to_all | solution.py:10
  19.4 12.2 %all_gather.7 = f32[32,8,4,128]{3,0,2,1:T(8,128)S(1)} all-gather(f32[8,8,4,128]{3,0,2,1:T(8,128)S(1)} %copy.135), channel_id=1, replica_groups=mesh['col'=4,'gx'=16,'gy'=8] {'col'}, dimensions={0}, use_global_device_ids=true | all-gather | bytes 655360 | tf_op jit(solution)/shard_map/all_gather | solution.py:91
  31.7 1.3 collective-permute-start.4
  33.0 1.3 collective-permute-start.5
  34.3 6.8 %all_gather.6 = f32[32,32,3,3,3]{1,0,4,3,2:T(8,128)S(1)} all-gather(f32[8,32,3,3,3]{1,0,4,3,2:T(8,128)S(1)} %copy-done.42), channel_id=1, replica_groups=mesh['col'=4,'gx'=16,'gy'=8] {'col'}, dimensions={0}, use_global_device_ids=true | all-gather | bytes 138240 | tf_op jit(solution)/shard_map/all_gather | solution.py:90
  44.9 1.3 collective-permute-start.6
  46.5 1.8 collective-permute-start.7
  48.3 1.4 fusion.120
  49.7 1.4 fusion.116
  66.7 4.0 collective-permute-start
  70.8 1.3 collective-permute-start.1
  73.1 3.3 collective-permute-done.1
  77.2 4.5 collective-permute-start.2
  82.0 1.5 collective-permute-start.3
  83.5 1.7 fusion.78
  85.3 1.7 convolution_bitcast_fusion
  88.1 1.2 copy.130
  89.3 1.3 copy.131
  90.6 2.1 select_maximum_fusion.2
  92.7 4.4 fusion.321
  97.1 1.9 fusion.216
  99.0 1.8 fusion.218
  100.8 1.8 fusion.220
  103.8 1.1 fusion.224
  106.0 1.1 fusion.228
  112.6 1.1 convolution_bitcast_fusion.2
  114.8 1.2 convolution_bitcast_fusion.4
  116.0 1.2 convolution_bitcast_fusion.5
  118.2 1.2 convolution_bitcast_fusion.7
  119.4 1.4 convolution_bitcast_fusion.8
  121.8 1.2 convolution_bitcast_fusion.10
  123.0 1.2 fusion.77
  124.1 1.2 fusion.76
  125.3 1.2 fusion.75
  126.4 1.2 fusion.74
  127.6 1.2 fusion.73
  128.7 1.2 fusion.72
  129.9 1.2 fusion.71
  131.1 1.2 fusion.70
  132.2 1.2 fusion.69
  133.4 1.2 fusion.68
  134.5 1.2 fusion.67
  135.7 1.2 fusion.66
  136.8 1.2 fusion.65
  139.1 1.2 fusion.63
  140.3 1.2 fusion.62
  141.4 1.2 fusion.61
  142.6 1.2 fusion.60
  143.8 1.2 fusion.59
  144.9 1.2 fusion.58
  147.2 1.1 fusion.56
  148.4 1.2 fusion.55
  149.6 1.1 fusion.54
  150.7 1.1 fusion.53
  151.9 1.1 fusion.52
  153.0 1.1 fusion.51
  154.2 1.7 copy.196
  155.9 1.7 broadcast_in_dim.8
  158.2 1.4 constant_dynamic-update-slice_fusion.3
  159.8 1.9 fusion.48
  161.6 1.7 fusion.11
  163.5 1.5 fusion.40
  165.7 457.6 %all-reduce.4.cloned.1.call-done = f32[4,54,128]{2,1,0:T(8,128)} async-done(((f32[4,54,128]{2,1,0:T(8,128)}), f32[4,54,128]{2,1,0:T(8,128)}) %all-reduce.4.cloned.1.call-update) | async-done | bytes 110608 | tf_op jit(solution)/shard_map/psum | solution.py:101
  624.9 1.6 copy.199
  (163 shorter events, 40.8 us)
Async XLA Ops:
  7.2 12.2 %copy-start = (f32[8,8,4,128]{3,2,1,0:T(4,128)S(1)}, f32[8,8,4,128]{3,2,1,0:T(4,128)}, u32[]{:S(2)}) copy-start(f32[8,8,4,128]{3,2,1,0:T(4,128)} %param.5) | copy-start | bytes 393220
  7.2 27.1 %copy-start.42 = (f32[8,32,3,3,3]{1,0,4,3,2:T(8,128)S(1)}, f32[8,32,3,3,3]{1,0,4,3,2:T(8,128)}, u32[]{:S(2)}) copy-start(f32[8,32,3,3,3]{1,0,4,3,2:T(8,128)} %param.4) | copy-start | bytes 82948
  9.1 57.6 %all-to-all-start = ((f32[4,8,8,4,128]{4,1,3,2,0:T(8,128)}), f32[4,8,8,4,128]{4,1,3,2,0:T(8,128)S(1)}, u32[]{:S(2)}, u32[]{:S(2)}) async-start(f32[4,8,8,4,128]{4,1,3,2,0:T(8,128)} %stack.91), calls=%async_computation | async-start | bytes 1048576 | tf_op jit(solution)/shard_map/all_to_all | solution.py:10
  19.4 604.0 %all-reduce.4.cloned.1.call-start = ((), (), s32[]{:S(2)}) async-start(), calls=%async_computation.1 | async-start | bytes 229376 | tf_op jit(solution)/shard_map/psum | solution.py:101
  31.7 10.6 %collective-permute-start.4 = (f32[32,8,1,128]{3,0,2,1:T(8,128)S(1)}, f32[32,8,1,128]{3,0,2,1:T(8,128)S(1)}, u32[]{:S(2)}, u32[]{:S(2)}) collective-permute-start(f32[32,8,1,128]{3,0,2,1:T(8,128)S(1)} %get-tuple-element.45), channel_id=1, source_target_pairs={{0,8},{8,16},{16,24},{24,32},{32,40},{40,48},{48,56},{56,64},{64,7... | collective-permute-start | bytes 393224 | tf_op jit(solution)/shard_map/ppermute | solution.py:19
  33.0 9.3 %collective-permute-start.5 = (f32[32,8,1,128]{3,0,2,1:T(8,128)S(1)}, f32[32,8,1,128]{3,0,2,1:T(8,128)S(1)}, u32[]{:S(2)}, u32[]{:S(2)}) collective-permute-start(f32[32,8,1,128]{3,0,2,1:T(8,128)S(1)} %get-tuple-element.44), channel_id=1, source_target_pairs={{8,0},{16,8},{24,16},{32,24},{40,32},{48,40},{56,48},{64,56},{72,6... | collective-permute-start | bytes 393224 | tf_op jit(solution)/shard_map/ppermute | solution.py:22
  41.2 1.1 copy-start.19
  42.3 0.7 copy-start.40
  42.9 0.6 copy-start.38
  44.9 6.2 collective-permute-start.6
  46.5 5.0 collective-permute-start.7
  51.8 1.0 copy-start.20
  60.4 3.1 copy-start.41
  66.7 6.4 %collective-permute-start = (f32[32,8,1,128]{3,0,2,1:T(8,128)S(1)}, f32[32,8,1,128]{3,0,2,1:T(8,128)S(1)}, u32[]{:S(2)}, u32[]{:S(2)}) collective-permute-start(f32[32,8,1,128]{3,0,2,1:T(8,128)S(1)} %get-tuple-element.46), channel_id=1, source_target_pairs={{0,8},{8,16},{16,24},{24,32},{32,40},{40,48},{48,56},{56,64},{64,7... | collective-permute-start | bytes 393224 | tf_op jit(solution)/shard_map/ppermute | solution.py:19
  70.8 5.7 collective-permute-start.1
  77.2 10.9 %collective-permute-start.2 = (f32[32,8,6,1]{0,1,3,2:T(8,128)S(1)}, f32[32,8,6,1]{0,1,3,2:T(8,128)S(1)}, u32[]{:S(2)}, u32[]{:S(2)}) collective-permute-start(f32[32,8,6,1]{0,1,3,2:T(8,128)S(1)} %copy.128), channel_id=1, source_target_pairs={{0,1},{1,2},{2,3},{3,4},{4,5},{5,6},{6,7},{8,9},{9,10},{10,11},{11... | collective-permute-start | bytes 18440 | tf_op jit(solution)/shard_map/ppermute | solution.py:19
  82.0 7.3 %collective-permute-start.3 = (f32[32,8,6,1]{0,1,3,2:T(8,128)S(1)}, f32[32,8,6,1]{0,1,3,2:T(8,128)S(1)}, u32[]{:S(2)}, u32[]{:S(2)}) collective-permute-start(f32[32,8,6,1]{0,1,3,2:T(8,128)S(1)} %copy.129), channel_id=1, source_target_pairs={{1,0},{2,1},{3,2},{4,3},{5,4},{6,5},{7,6},{9,8},{10,9},{11,10},{12... | collective-permute-start | bytes 18440 | tf_op jit(solution)/shard_map/ppermute | solution.py:22
  97.1 5.6 copy-start.43
  100.8 7.5 %copy-start.3 = (f32[32,8,6,1]{3,0,2,1:T(8,128)S(1)}, f32[32,8,6,1]{3,0,2,1:T(8,128)}, u32[]{:S(2)}) copy-start(f32[32,8,6,1]{3,0,2,1:T(8,128)} %copy.130) | copy-start | bytes 18436
  100.8 7.5 %copy-start.4 = (f32[32,8,6,1]{3,0,2,1:T(8,128)S(1)}, f32[32,8,6,1]{3,0,2,1:T(8,128)}, u32[]{:S(2)}) copy-start(f32[32,8,6,1]{3,0,2,1:T(8,128)} %copy.131) | copy-start | bytes 18436
  108.9 2.1 copy-start.1
  109.0 12.8 %copy-start.2 = (f32[32,8,6,129]{3,0,2,1:T(8,128)}, f32[32,8,6,129]{3,0,2,1:T(8,128)S(1)}, u32[]{:S(2)}) copy-start(f32[32,8,6,129]{3,0,2,1:T(8,128)S(1)} %get-tuple-element.39) | copy-start | bytes 2377732
  116.0 7.0 %copy-start.18 = (f32[32,8,4,128]{3,0,2,1:T(8,128)S(1)}, f32[32,8,4,128]{3,0,2,1:T(8,128)}, u32[]{:S(2)}) copy-start(f32[32,8,4,128]{3,0,2,1:T(8,128)} %get-tuple-element.29) | copy-start | bytes 1572868
  117.2 7.0 %copy-start.17 = (f32[32,8,4,128]{3,0,2,1:T(8,128)S(1)}, f32[32,8,4,128]{3,0,2,1:T(8,128)}, u32[]{:S(2)}) copy-start(f32[32,8,4,128]{3,0,2,1:T(8,128)} %get-tuple-element.28) | copy-start | bytes 1572868
  118.2 7.1 %copy-start.16 = (f32[32,8,4,128]{3,0,2,1:T(8,128)S(1)}, f32[32,8,4,128]{3,0,2,1:T(8,128)}, u32[]{:S(2)}) copy-start(f32[32,8,4,128]{3,0,2,1:T(8,128)} %get-tuple-element.27) | copy-start | bytes 1572868
  119.4 7.0 %copy-start.15 = (f32[32,8,4,128]{3,0,2,1:T(8,128)S(1)}, f32[32,8,4,128]{3,0,2,1:T(8,128)}, u32[]{:S(2)}) copy-start(f32[32,8,4,128]{3,0,2,1:T(8,128)} %get-tuple-element.26) | copy-start | bytes 1572868
  120.7 6.8 %copy-start.14 = (f32[32,8,4,128]{3,0,2,1:T(8,128)S(1)}, f32[32,8,4,128]{3,0,2,1:T(8,128)}, u32[]{:S(2)}) copy-start(f32[32,8,4,128]{3,0,2,1:T(8,128)} %get-tuple-element.25) | copy-start | bytes 1572868
  121.8 7.0 %copy-start.13 = (f32[32,8,4,128]{3,0,2,1:T(8,128)S(1)}, f32[32,8,4,128]{3,0,2,1:T(8,128)}, u32[]{:S(2)}) copy-start(f32[32,8,4,128]{3,0,2,1:T(8,128)} %get-tuple-element.24) | copy-start | bytes 1572868
  122.9 7.0 %copy-start.12 = (f32[32,8,4,128]{3,0,2,1:T(8,128)S(1)}, f32[32,8,4,128]{3,0,2,1:T(8,128)}, u32[]{:S(2)}) copy-start(f32[32,8,4,128]{3,0,2,1:T(8,128)} %get-tuple-element.23) | copy-start | bytes 1572868
  124.1 7.0 %copy-start.11 = (f32[32,8,4,128]{3,0,2,1:T(8,128)S(1)}, f32[32,8,4,128]{3,0,2,1:T(8,128)}, u32[]{:S(2)}) copy-start(f32[32,8,4,128]{3,0,2,1:T(8,128)} %get-tuple-element.22) | copy-start | bytes 1572868
  125.3 6.9 %copy-start.10 = (f32[32,8,4,128]{3,0,2,1:T(8,128)S(1)}, f32[32,8,4,128]{3,0,2,1:T(8,128)}, u32[]{:S(2)}) copy-start(f32[32,8,4,128]{3,0,2,1:T(8,128)} %get-tuple-element.21) | copy-start | bytes 1572868
  127.6 6.9 %copy-start.9 = (f32[32,8,4,128]{3,0,2,1:T(8,128)S(1)}, f32[32,8,4,128]{3,0,2,1:T(8,128)}, u32[]{:S(2)}) copy-start(f32[32,8,4,128]{3,0,2,1:T(8,128)} %get-tuple-element.43) | copy-start | bytes 1572868
  134.5 6.9 %copy-start.5 = (f32[32,8,4,128]{3,0,2,1:T(8,128)S(1)}, f32[32,8,4,128]{3,0,2,1:T(8,128)}, u32[]{:S(2)}) copy-start(f32[32,8,4,128]{3,0,2,1:T(8,128)} %get-tuple-element.42) | copy-start | bytes 1572868
  136.8 6.9 %copy-start.8 = (f32[32,8,4,128]{3,0,2,1:T(8,128)S(1)}, f32[32,8,4,128]{3,0,2,1:T(8,128)}, u32[]{:S(2)}) copy-start(f32[32,8,4,128]{3,0,2,1:T(8,128)} %get-tuple-element.20) | copy-start | bytes 1572868
  138.0 6.9 %copy-start.7 = (f32[32,8,4,128]{3,0,2,1:T(8,128)S(1)}, f32[32,8,4,128]{3,0,2,1:T(8,128)}, u32[]{:S(2)}) copy-start(f32[32,8,4,128]{3,0,2,1:T(8,128)} %get-tuple-element.19) | copy-start | bytes 1572868
  139.1 6.9 %copy-start.6 = (f32[32,8,4,128]{3,0,2,1:T(8,128)S(1)}, f32[32,8,4,128]{3,0,2,1:T(8,128)}, u32[]{:S(2)}) copy-start(f32[32,8,4,128]{3,0,2,1:T(8,128)} %get-tuple-element.18) | copy-start | bytes 1572868
  148.4 11.2 %copy-start.21 = (f32[8,4,128,8]{2,3,1,0:T(8,128)S(1)}, f32[8,4,128,8]{2,3,1,0:T(8,128)}, u32[]{:S(2)}) copy-start(f32[8,4,128,8]{2,3,1,0:T(8,128)} %fusion.216) | copy-start | bytes 393220
  148.4 11.3 %copy-start.22 = (f32[8,4,128,8]{2,3,1,0:T(8,128)S(1)}, f32[8,4,128,8]{2,3,1,0:T(8,128)}, u32[]{:S(2)}) copy-start(f32[8,4,128,8]{2,3,1,0:T(8,128)} %fusion.218) | copy-start | bytes 393220
  148.4 11.3 %copy-start.23 = (f32[8,4,128,8]{2,3,1,0:T(8,128)S(1)}, f32[8,4,128,8]{2,3,1,0:T(8,128)}, u32[]{:S(2)}) copy-start(f32[8,4,128,8]{2,3,1,0:T(8,128)} %fusion.220) | copy-start | bytes 393220
  148.4 11.3 %copy-start.24 = (f32[8,4,128,8]{2,3,1,0:T(8,128)S(1)}, f32[8,4,128,8]{2,3,1,0:T(8,128)}, u32[]{:S(2)}) copy-start(f32[8,4,128,8]{2,3,1,0:T(8,128)} %fusion.222) | copy-start | bytes 393220
  148.4 11.3 %copy-start.25 = (f32[8,4,128,8]{2,3,1,0:T(8,128)S(1)}, f32[8,4,128,8]{2,3,1,0:T(8,128)}, u32[]{:S(2)}) copy-start(f32[8,4,128,8]{2,3,1,0:T(8,128)} %fusion.224) | copy-start | bytes 393220
  148.4 11.3 %copy-start.26 = (f32[8,4,128,8]{2,3,1,0:T(8,128)S(1)}, f32[8,4,128,8]{2,3,1,0:T(8,128)}, u32[]{:S(2)}) copy-start(f32[8,4,128,8]{2,3,1,0:T(8,128)} %fusion.226) | copy-start | bytes 393220
  148.4 11.3 %copy-start.27 = (f32[8,4,128,8]{2,3,1,0:T(8,128)S(1)}, f32[8,4,128,8]{2,3,1,0:T(8,128)}, u32[]{:S(2)}) copy-start(f32[8,4,128,8]{2,3,1,0:T(8,128)} %fusion.228) | copy-start | bytes 393220
  148.4 11.3 %copy-start.28 = (f32[8,4,128,8]{2,3,1,0:T(8,128)S(1)}, f32[8,4,128,8]{2,3,1,0:T(8,128)}, u32[]{:S(2)}) copy-start(f32[8,4,128,8]{2,3,1,0:T(8,128)} %fusion.230) | copy-start | bytes 393220
  154.2 9.2 %copy-start.29 = (f32[8,8,4,128]{3,0,2,1:T(8,128)S(1)}, f32[8,8,4,128]{3,0,2,1:T(8,128)}, u32[]{:S(2)}) copy-start(f32[8,8,4,128]{3,0,2,1:T(8,128)} %convolution_bitcast_fusion.2) | copy-start | bytes 393220
  159.7 3.7 copy-start.30
  159.7 3.7 copy-start.31
  159.7 3.7 copy-start.32
  159.7 3.7 copy-start.33
  159.7 3.7 copy-start.34
  159.7 3.7 copy-start.35
  159.7 3.7 copy-start.36
  159.8 3.7 copy-start.37
  159.8 3.7 copy-start.39
Sparse Core Ops, SparseCore 0:
  159.7 463.5 all-reduce.3
